TPU v7x, 256 devices: a whole 4x4x8 slice. The times are simulated.
256 devices in a mesh: seq: 16 (over x, z_lo, core), hid: 16 (over z_hi, y).
Axes of the slice: x: 4, y: 4, z: 8 (z_hi: 4, z_lo: 2; z = z_hi * 2 + z_lo), core: 2. Of those that a mesh axis runs over, the one named last changes fastest.
Arguments:
- stream: bfloat16 [8192, 2048], P('seq'), may hold values from -5 to 5
- queries: bfloat16 [8192, 16, 128], P('seq', 'hid'), may hold values from -150 to 150
- key_rows: bfloat16 [8192, 16, 128], P('seq', 'hid'), may hold values from -5 to 5
- value_rows: bfloat16 [8192, 16, 128], P('seq', 'hid'), may hold values from -5 to 5
- segment_ids: int32 [8192], replicated, may hold values from 0 to 3, never falling along the last dimension, each value on 1 to 4096 neighbouring positions
- out_proj: bfloat16 [16, 128, 2048], P('hid'), may hold values from -0.125 to 0.125
- norm_gain: float32 [2048], replicated, may hold values from 0.1 to 1.9
- expert_ids: int32 [8192, 6], P('seq'), may hold values from 0 to 63, all different within a row; in each aligned block of 512 rows (0 to 511, 512 to 1023, ...) at most 64 rows name the same one
- route_gates: float32 [8192, 6], P('seq'), may hold values from 0.05 to 0.4
- gate_proj: bfloat16 [90112, 2048], P(('seq', 'hid')), may hold values from -0.125 to 0.125
- up_proj: bfloat16 [90112, 2048], P(('seq', 'hid')), may hold values from -0.125 to 0.125
- down_proj: bfloat16 [90112, 2048], P(('seq', 'hid')), may hold values from -0.15625 to 0.15625
- shared_gate: bfloat16 [2816, 2048], P('hid'), may hold values from -0.125 to 0.125
- shared_up: bfloat16 [2816, 2048], P('hid'), may hold values from -0.125 to 0.125
- shared_down: bfloat16 [2816, 2048], P('hid'), may hold values from -0.109375 to 0.109375
Outputs:
- layer_out: bfloat16 [8192, 2048], P('seq', 'hid')
Inputs may be any that keep to these rules, and one draw needn't show every extreme that they name: `segment_ids`: segment numbers never fall along the tokens; every segment has at most 4096 tokens and one has exactly 4096. `expert_ids`: the 6 experts of a token differ; among the 512 tokens of one index of seq no expert is named by more than 64 tokens, a bound that some block reaches of them.
All inputs are finite; a program needn't handle non-finite values.
Results may differ from a plain program's by a relative error of at most 0.019.
Values may be sent and summed in bfloat16 or wider, within the bound.
No kernel may reach another device: no remote copies, remote signals or barrier semaphores. Data moves between devices by JAX's collectives and lax.ppermute only.
A program may use at most 128 MiB of HBM per device.

v0:
```python
import jax
import jax.numpy as jnp
from jax import lax
from jax.sharding import PartitionSpec as P

EXPERTS = 64
FF = 1408
TOP = 6
CAP = 64
LONGEST = 4096


def seq_gather(rows, seq_count):
    spread = jnp.broadcast_to(rows[None], (seq_count,) + rows.shape)
    got = lax.all_to_all(spread, "seq", split_axis=0, concat_axis=0, tiled=True)
    return got.reshape((seq_count * rows.shape[0],) + rows.shape[1:])


def hid_scatter_sum(part, hid_count):
    rows, width = part.shape
    got = lax.all_to_all(
        part.reshape(rows, hid_count, width // hid_count),
        "hid",
        split_axis=1,
        concat_axis=1,
        tiled=True,
    )
    return jnp.sum(got.astype(jnp.float32), axis=1)


def hid_permute_sum(part, hid_count, hid_index):
    rows, width = part.shape
    chunks = part.reshape(rows, hid_count, width // hid_count)
    total = lax.dynamic_index_in_dim(chunks, hid_index, 1, keepdims=False).astype(jnp.float32)
    for shift in range(1, hid_count):
        sent = lax.dynamic_index_in_dim(chunks, (hid_index + shift) % hid_count, 1, keepdims=False)
        pairs = [(i, (i + shift) % hid_count) for i in range(hid_count)]
        total = total + lax.ppermute(sent, "hid", pairs).astype(jnp.float32)
    return total


def on_device(
    stream,
    queries,
    key_rows,
    value_rows,
    segment_ids,
    out_proj,
    norm_gain,
    expert_ids,
    route_gates,
    gate_proj,
    up_proj,
    down_proj,
    shared_gate,
    shared_up,
    shared_down,
):
    tok_count = queries.shape[0]
    local_heads = queries.shape[1]
    head_width = queries.shape[2]
    width = stream.shape[1]
    inv_root = head_width ** (-0.5)
    seq_count = lax.axis_size("seq")
    hid_count = lax.axis_size("hid")
    hid_index = lax.axis_index("hid")
    query_first = lax.axis_index("seq") * tok_count
    query_seg = lax.dynamic_slice_in_dim(segment_ids, query_first, tok_count)
    query_pos = query_first + jnp.arange(tok_count, dtype=jnp.int32)
    run_max = jnp.full((tok_count, local_heads), -1e30, jnp.float32)
    window = min(seq_count, -(-LONGEST // tok_count) + 1)
    both = jnp.concatenate([key_rows, value_rows], axis=1)
    blocks = [both]
    for shift in range(1, window):
        pairs = [(i, i + shift) for i in range(seq_count - shift)]
        blocks.append(lax.ppermute(both, "seq", pairs))
    both_win = jnp.concatenate(blocks[::-1], axis=0)
    key_part = both_win[:, :local_heads]
    value_part = both_win[:, local_heads:]
    row_count = key_part.shape[0]
    key_first = query_first - (window - 1) * tok_count
    key_pos = key_first + jnp.arange(row_count, dtype=jnp.int32)
    seg_padded = jnp.concatenate(
        [jnp.full(((window - 1) * tok_count,), -1, jnp.int32), segment_ids]
    )
    key_seg = lax.dynamic_slice_in_dim(seg_padded, query_first, row_count)
    scores = (
        jnp.einsum("qhd,khd->qhk", queries, key_part, preferred_element_type=jnp.float32) * inv_root
    )
    allowed = (query_seg[:, None] == key_seg[None, :]) & (key_pos[None, :] <= query_pos[:, None])
    scores = jnp.where(allowed[:, None, :], scores, -1e30)
    new_max = jnp.maximum(run_max, jnp.max(scores, axis=2))
    weights = jnp.where(allowed[:, None, :], jnp.exp(scores - new_max[:, :, None]), 0.0)
    new_sum = jnp.sum(weights, axis=2)
    probs = weights.astype(jnp.bfloat16)
    new_acc = jnp.einsum("qhk,khd->qhd", probs, value_part, preferred_element_type=jnp.float32)
    attended = (
        (new_acc / new_sum[:, :, None])
        .astype(jnp.bfloat16)
        .reshape(tok_count, local_heads * head_width)
    )
    out_flat = out_proj.reshape(local_heads * head_width, width)
    partial_mix = jnp.dot(attended, out_flat, preferred_element_type=jnp.float32)
    col_count = width // hid_count
    col_first = hid_index * col_count
    mixed_cols = lax.dynamic_slice_in_dim(stream, col_first, col_count, 1).astype(
        jnp.float32
    ) + hid_scatter_sum(partial_mix.astype(jnp.bfloat16), hid_count)
    mixed_all = (
        lax.all_to_all(
            jnp.broadcast_to(
                mixed_cols.astype(jnp.bfloat16)[:, None, :], (tok_count, hid_count, col_count)
            ),
            "hid",
            split_axis=1,
            concat_axis=1,
            tiled=True,
        )
        .reshape(tok_count, width)
        .astype(jnp.float32)
    )
    mean_square = jnp.mean(mixed_all * mixed_all, axis=1, keepdims=True)
    normed = (mixed_all * lax.rsqrt(mean_square + 1e-06) * norm_gain).astype(jnp.bfloat16)
    shared_gate_val = jnp.einsum(
        "td,fd->tf", normed, shared_gate, preferred_element_type=jnp.float32
    )
    shared_up_val = jnp.einsum("td,fd->tf", normed, shared_up, preferred_element_type=jnp.float32)
    shared_act = (jax.nn.silu(shared_gate_val) * shared_up_val).astype(jnp.bfloat16)
    shared_part = jnp.dot(shared_act, shared_down, preferred_element_type=jnp.float32)
    shared_out = hid_scatter_sum(shared_part.astype(jnp.bfloat16), hid_count)
    unit_rows = gate_proj.shape[0]
    held_count = max(1, unit_rows // FF)
    held_units = unit_rows // held_count
    local_experts = EXPERTS // seq_count
    first_local = hid_index * unit_rows // FF
    flat_ids = expert_ids.reshape(-1)
    onehot = (flat_ids[:, None] == jnp.arange(EXPERTS, dtype=jnp.int32)[None, :]).astype(jnp.int32)
    slot_rank = jnp.sum((jnp.cumsum(onehot, axis=0) - 1) * onehot, axis=1)
    owner_group = flat_ids // local_experts
    local_expert = flat_ids % local_experts
    held_offset = local_expert - first_local
    is_held = (held_offset >= 0) & (held_offset < held_count)
    slot_total = seq_count * held_count * CAP
    send_index = jnp.where(
        is_held, (owner_group * held_count + held_offset) * CAP + slot_rank, slot_total
    )
    route_token = jnp.arange(tok_count * TOP, dtype=jnp.int32) // TOP
    slot_token = jnp.full((slot_total,), -1, jnp.int32).at[send_index].set(route_token, mode="drop")
    send_rows = jnp.where(
        (slot_token >= 0)[:, None], normed[jnp.maximum(slot_token, 0)], jnp.zeros((), jnp.bfloat16)
    )
    send_rows = send_rows.reshape(seq_count, held_count, CAP, width)
    received = lax.all_to_all(send_rows, "seq", split_axis=0, concat_axis=0, tiled=True)
    gate_local = gate_proj.reshape(held_count, held_units, width)
    up_local = up_proj.reshape(held_count, held_units, width)
    down_local = down_proj.reshape(held_count, held_units, hid_count, col_count)
    gate_val = jnp.einsum(
        "sicd,ifd->sicf", received, gate_local, preferred_element_type=jnp.float32
    )
    up_val = jnp.einsum("sicd,ifd->sicf", received, up_local, preferred_element_type=jnp.float32)
    expert_act = (jax.nn.silu(gate_val) * up_val).astype(jnp.bfloat16)
    down_part = jnp.einsum(
        "sicf,ifnx->niscx", expert_act, down_local, preferred_element_type=jnp.float32
    ).astype(jnp.bfloat16)
    down_part = down_part.reshape(hid_count, held_count, seq_count * CAP, col_count)
    peer_parts = lax.all_to_all(down_part, "hid", split_axis=0, concat_axis=0, tiled=True)
    part_count = hid_count * held_count // local_experts
    expert_out = jnp.sum(
        peer_parts.reshape(local_experts, part_count, seq_count * CAP, col_count).astype(
            jnp.float32
        ),
        axis=1,
    ).astype(jnp.bfloat16)
    returned = lax.all_to_all(
        expert_out.reshape(local_experts, seq_count, CAP, col_count),
        "seq",
        split_axis=1,
        concat_axis=1,
        tiled=True,
    ).reshape(-1, col_count)
    pick_index = local_expert * (seq_count * CAP) + owner_group * CAP + slot_rank
    picked = returned[pick_index].reshape(tok_count, TOP, col_count)
    routed_sum = jnp.einsum("tj,tjd->td", route_gates, picked.astype(jnp.float32))
    return (mixed_cols + shared_out + routed_sum).astype(jnp.bfloat16)


def solution(mesh):
    placed = (
        P("seq", None),
        P("seq", "hid", None),
        P("seq", "hid", None),
        P("seq", "hid", None),
        P(),
        P("hid", None, None),
        P(),
        P("seq", None),
        P("seq", None),
        P(("seq", "hid"), None),
        P(("seq", "hid"), None),
        P(("seq", "hid"), None),
        P("hid", None),
        P("hid", None),
        P("hid", None),
    )
    return jax.shard_map(
        on_device, mesh=mesh, in_specs=placed, out_specs=P("seq", "hid"), check_vma=False
    )
```

profile of v0, /device:TPU:64, one launch (start us, length us, event | category | flops | bytes accessed | tf_op | source)
XLA Modules:
  0.0 507.8 jit_solution(17655521724245121680)
XLA Ops:
  2.0 4.9 collective-permute-start
  7.0 3.0 collective-permute-start.1
  10.0 2.1 collective-permute-start.2
  13.5 1.6 collective-permute-start.4
  16.7 8.2 %collective-permute-done = bf16[512,2,128]{2,0,1:T(8,128)(2,1)S(1)} collective-permute-done((bf16[512,2,128]{2,0,1:T(8,128)(2,1)S(1)}, bf16[512,2,128]{2,0,1:T(8,128)(2,1)S(1)}, u32[]{:S(2)}, u32[]{:S(2)}) %collective-permute-start) | collective-permute-done | bytes 262176 | tf_op jit(solution)/shard_map/ppermute | solution.py:76
  24.9 2.0 collective-permute-start.5
  27.0 3.9 collective-permute-start.6
  30.9 3.8 collective-permute-start.7
  34.7 7.1 %collective-permute-done.3 = bf16[512,2,128]{2,0,1:T(8,128)(2,1)S(1)} collective-permute-done((bf16[512,2,128]{2,0,1:T(8,128)(2,1)S(1)}, bf16[512,2,128]{2,0,1:T(8,128)(2,1)S(1)}, u32[]{:S(2)}, u32[]{:S(2)}) %collective-permute-start.3) | collective-permute-done | bytes 262176 | tf_op jit(solution)/shard_map/ppermute | solution.py:76
  41.8 5.6 %collective-permute-done.4 = bf16[512,2,128]{2,0,1:T(8,128)(2,1)S(1)} collective-permute-done((bf16[512,2,128]{2,0,1:T(8,128)(2,1)S(1)}, bf16[512,2,128]{2,0,1:T(8,128)(2,1)S(1)}, u32[]{:S(2)}, u32[]{:S(2)}) %collective-permute-start.4) | collective-permute-done | bytes 262176 | tf_op jit(solution)/shard_map/ppermute | solution.py:76
  47.7 2.2 fusion
  49.9 3.6 copy-done.2
  53.5 4.1 fusion.1
  57.6 8.1 %fusion.13 = bf16[64,16,8,128]{3,2,1,0:T(8,128)(2,1)S(1)} fusion(f32[4608,512]{1,0:T(8,128)} %copy-done.2, f32[512]{0:T(512)S(1)} %broadcast_maximum_fusion, s32[512]{0:T(512)S(1)} %iota_add_fusion.1, s32[512]{0:T(512)S(1)} %dynamic_slice.10, s32[4608]{0:T(1024)} %copy-done.11, s32[4608]{0:T(1024)} %copy-done.10, bf16[4608,2,128]{2,0,1:T(8,128)(2,1)} %copy-done.14, ...), kind=kOutput, calls=%fused_computation.30 | convolution fusion | flops 892469248 | bytes 13287424 | tf_op jit(solution)/shard_map/dot_general | solution.py:103
  65.7 1.9 copy.69
  67.6 10.8 %all-to-all-start = ((bf16[512,16,128]{2,0,1:T(8,128)(2,1)}), bf16[512,16,128]{2,0,1:T(8,128)(2,1)S(1)}, u32[]{:S(2)}, u32[]{:S(2)}) async-start(bf16[512,16,128]{2,0,1:T(8,128)(2,1)} %bitcast.219), calls=%async_computation | async-start | bytes 4194304 | tf_op jit(solution)/shard_map/all_to_all | solution.py:21
  78.3 44.6 %all-to-all-done = bf16[512,16,128]{2,0,1:T(8,128)(2,1)S(1)} async-done(((bf16[512,16,128]{2,0,1:T(8,128)(2,1)}), bf16[512,16,128]{2,0,1:T(8,128)(2,1)S(1)}, u32[]{:S(2)}, u32[]{:S(2)}) %all-to-all-start) | async-done | bytes 2097184 | tf_op jit(solution)/shard_map/all_to_all | solution.py:21
  124.9 1.7 broadcast_in_dim.58
  126.6 8.0 %all-to-all-start.1 = ((bf16[512,16,128]{2,0,1:T(8,128)(2,1)}), bf16[512,16,128]{2,0,1:T(8,128)(2,1)S(1)}, u32[]{:S(2)}, u32[]{:S(2)}) async-start(bf16[512,16,128]{2,0,1:T(8,128)(2,1)} %broadcast_in_dim.58), calls=%async_computation.1 | async-start | bytes 4194304 | tf_op jit(solution)/shard_map/all_to_all | solution.py:110
  135.4 1.7 eq.54
  137.1 1.7 eq.50
  140.0 1.6 fusion.50
  141.6 34.8 %reduce-window.6 = s32[64,24,128]{2,1,0:T(8,128)} reduce-window(s32[64,24,128]{2,1,0:T(8,128)} %fusion.50, s32[]{:T(128)} %constant.41.clone.1), window={size=1x1x128 pad=0_0x0_0x127_0}, to_apply=%region_5.6 | reduce-window | flops 24969216 | bytes 1572868 | tf_op jit(solution)/shard_map/reduce-window
  176.5 2.3 slice.22
  178.8 2.2 copy.54
  186.2 12.1 %scatter_custom_fusion = s32[1024]{0:T(1024)S(1)} fusion(s32[3072]{0:T(1024)S(1)} %bitcast.230, s32[3072]{0:T(1024)} %add_select_fusion, s32[]{:T(128)} %constant.86.clone.1), kind=kCustom, calls=%fused_computation.105 | custom fusion | bytes 4608 | tf_op jit(solution)/shard_map/scatter | solution.py:148
  199.8 2.1 fusion.8
  201.9 6.0 %gather_fusion = bf16[1024,2048]{1,0:T(8,128)(2,1)} fusion(bf16[512,2048]{1,0:T(8,128)(2,1)S(1)} %fusion.8, s32[1024]{0:T(1024)S(1)} %maximum_clamp_fusion), kind=kCustom, calls=%fused_computation | custom fusion | bytes 8392704 | tf_op jit(solution)/shard_map/gather | solution.py:150
  207.9 2.5 broadcast_select_fusion
  210.5 56.2 %all_to_all.30 = bf16[16,1,64,2048]{3,2,1,0:T(8,128)(2,1)S(1)} all-to-all(bf16[16,1,64,2048]{3,2,1,0:T(8,128)(2,1)S(1)} %broadcast_select_fusion), channel_id=1, replica_groups=mesh['seq'=16,'hid'=16] {'seq'}, dimensions={0} | all-to-all | bytes 8388608 | tf_op jit(solution)/shard_map/all_to_all | solution.py:153
  266.7 1.9 copy-done.3
  268.6 3.5 fusion.11
  272.2 8.4 %convert_bitcast_fusion.1 = bf16[16,1,16,64,128]{4,3,0,2,1:T(8,128)(2,1)} fusion(bf16[352,2048]{1,0:T(8,128)(2,1)S(1)} %copy-done, bf16[16,1,64,2048]{3,2,1,0:T(8,128)(2,1)} %copy-done.3, f32[16,64,352]{2,1,0:T(8,128)} %fusion.11, bf16[352,2048]{1,0:T(8,128)(2,1)} %param.26), kind=kOutput, calls=%fused_computation.22 | convolution fusion | flops 2957049856 | bytes 12713984 | tf_op jit(solution)/shard_map/sicf,ifnx->niscx/dot_general | solution.py:162
  280.6 5.5 %copy.47 = bf16[16,1,16,64,128]{4,3,2,0,1:T(8,128)(2,1)} copy(bf16[16,1,16,64,128]{4,3,0,2,1:T(8,128)(2,1)} %convert_bitcast_fusion.1) | data formatting | bytes 8388608 | tf_op jit(solution)/shard_map/convert_element_type | solution.py:164
  286.1 9.6 %all-to-all-start.4 = ((bf16[16,1,1024,128]{3,2,1,0:T(8,128)(2,1)}), bf16[16,1,1024,128]{3,2,1,0:T(8,128)(2,1)}, u32[]{:S(2)}, u32[]{:S(2)}) async-start(bf16[16,1,1024,128]{3,2,1,0:T(8,128)(2,1)} %bitcast.218), calls=%async_computation.4 | async-start | bytes 8388608 | tf_op jit(solution)/shard_map/all_to_all | solution.py:166
  295.7 2.7 fusion.76
  298.4 4.4 fusion.14
  302.8 3.5 copy.68
  306.3 78.1 %all-to-all-done.4 = bf16[16,1,1024,128]{3,2,1,0:T(8,128)(2,1)} async-done(((bf16[16,1,1024,128]{3,2,1,0:T(8,128)(2,1)}), bf16[16,1,1024,128]{3,2,1,0:T(8,128)(2,1)}, u32[]{:S(2)}, u32[]{:S(2)}) %all-to-all-start.4) | async-done | bytes 4194336 | tf_op jit(solution)/shard_map/all_to_all | solution.py:166
  384.5 13.2 %all-to-all-start.2 = ((bf16[512,16,128]{2,0,1:T(8,128)(2,1)}), bf16[512,16,128]{2,0,1:T(8,128)(2,1)S(1)}, u32[]{:S(2)}, u32[]{:S(2)}) async-start(bf16[512,16,128]{2,0,1:T(8,128)(2,1)} %bitcast.220), calls=%async_computation.2 | async-start | bytes 4194304 | tf_op jit(solution)/shard_map/all_to_all | solution.py:21
  397.6 2.9 bitcast_reduce_fusion
  401.6 28.3 %all-to-all-done.2 = bf16[512,16,128]{2,0,1:T(8,128)(2,1)S(1)} async-done(((bf16[512,16,128]{2,0,1:T(8,128)(2,1)}), bf16[512,16,128]{2,0,1:T(8,128)(2,1)S(1)}, u32[]{:S(2)}, u32[]{:S(2)}) %all-to-all-start.2) | async-done | bytes 2097184 | tf_op jit(solution)/shard_map/all_to_all | solution.py:21
  429.8 46.1 %all-to-all-start.5 = ((bf16[4,16,64,128]{3,2,0,1:T(8,128)(2,1)}), bf16[4,16,64,128]{3,2,0,1:T(8,128)(2,1)}, u32[]{:S(2)}, u32[]{:S(2)}) async-start(bf16[4,16,64,128]{3,2,0,1:T(8,128)(2,1)} %copy.49), calls=%async_computation.5 | async-start | bytes 2097152 | tf_op jit(solution)/shard_map/all_to_all | solution.py:174
  476.0 1.7 copy.52
  479.2 13.3 %all-to-all-done.5 = bf16[4,16,64,128]{3,2,0,1:T(8,128)(2,1)} async-done(((bf16[4,16,64,128]{3,2,0,1:T(8,128)(2,1)}), bf16[4,16,64,128]{3,2,0,1:T(8,128)(2,1)}, u32[]{:S(2)}, u32[]{:S(2)}) %all-to-all-start.5) | async-done | bytes 1048608 | tf_op jit(solution)/shard_map/all_to_all | solution.py:174
  493.9 9.2 %gather_fusion.1 = bf16[3072,128]{1,0:T(8,128)(2,1)S(1)} fusion(bf16[4096,128]{1,0:T(8,128)(2,1)S(1)} %bitcast.216, s32[3072]{0:T(1024)S(1)} %copy-done.13), kind=kCustom, calls=%fused_computation.1 | custom fusion | bytes 1585152 | tf_op jit(solution)/shard_map/gather | solution.py:182
  504.3 1.9 fusion.77
  506.2 1.6 add_convert_fusion
  (77 shorter events, 21.0 us)
Async XLA Ops:
  0.0 272.2 %copy-start = (bf16[352,2048]{1,0:T(8,128)(2,1)S(1)}, bf16[352,2048]{1,0:T(8,128)(2,1)}, u32[]{:S(2)}) copy-start(bf16[352,2048]{1,0:T(8,128)(2,1)} %param.25) | copy-start | bytes 4325380
  0.0 47.6 %copy-start.7 = (bf16[512,1,128]{2,0,1:T(8,128)(2,1)S(1)}, bf16[512,1,128]{2,0,1:T(8,128)(2,1)}, u32[]{:S(2)}) copy-start(bf16[512,1,128]{2,0,1:T(8,128)(2,1)} %param.17) | copy-start | bytes 393220
  1.0 46.6 %copy-start.8 = (bf16[512,1,128]{2,0,1:T(8,128)(2,1)S(1)}, bf16[512,1,128]{2,0,1:T(8,128)(2,1)}, u32[]{:S(2)}) copy-start(bf16[512,1,128]{2,0,1:T(8,128)(2,1)} %param.18) | copy-start | bytes 393220
  2.0 22.9 %collective-permute-start = (bf16[512,2,128]{2,0,1:T(8,128)(2,1)S(1)}, bf16[512,2,128]{2,0,1:T(8,128)(2,1)S(1)}, u32[]{:S(2)}, u32[]{:S(2)}) collective-permute-start(bf16[512,2,128]{2,0,1:T(8,128)(2,1)S(1)} %constant_dynamic-update-slice_fusion), channel_id=1, source_target_pairs={{0,128},{16,144},{32,160},{48,176},{64,192},{80,208},{96,224},{112... | collective-permute-start | bytes 786440 | tf_op jit(solution)/shard_map/ppermute | solution.py:76
  7.0 20.0 %collective-permute-start.1 = (bf16[512,2,128]{2,0,1:T(8,128)(2,1)S(1)}, bf16[512,2,128]{2,0,1:T(8,128)(2,1)S(1)}, u32[]{:S(2)}, u32[]{:S(2)}) collective-permute-start(bf16[512,2,128]{2,0,1:T(8,128)(2,1)S(1)} %constant_dynamic-update-slice_fusion), channel_id=1, source_target_pairs={{0,112},{16,128},{32,144},{48,160},{64,176},{80,192},{96,208},{112... | collective-permute-start | bytes 786440 | tf_op jit(solution)/shard_map/ppermute | solution.py:76
  10.0 20.9 %collective-permute-start.2 = (bf16[512,2,128]{2,0,1:T(8,128)(2,1)S(1)}, bf16[512,2,128]{2,0,1:T(8,128)(2,1)S(1)}, u32[]{:S(2)}, u32[]{:S(2)}) collective-permute-start(bf16[512,2,128]{2,0,1:T(8,128)(2,1)S(1)} %constant_dynamic-update-slice_fusion), channel_id=1, source_target_pairs={{0,96},{16,112},{32,128},{48,144},{64,160},{80,176},{96,192},{112,... | collective-permute-start | bytes 786440 | tf_op jit(solution)/shard_map/ppermute | solution.py:76
  12.2 29.6 %collective-permute-start.3 = (bf16[512,2,128]{2,0,1:T(8,128)(2,1)S(1)}, bf16[512,2,128]{2,0,1:T(8,128)(2,1)S(1)}, u32[]{:S(2)}, u32[]{:S(2)}) collective-permute-start(bf16[512,2,128]{2,0,1:T(8,128)(2,1)S(1)} %constant_dynamic-update-slice_fusion), channel_id=1, source_target_pairs={{0,80},{16,96},{32,112},{48,128},{64,144},{80,160},{96,176},{112,1... | collective-permute-start | bytes 786440 | tf_op jit(solution)/shard_map/ppermute | solution.py:76
  13.5 33.9 %collective-permute-start.4 = (bf16[512,2,128]{2,0,1:T(8,128)(2,1)S(1)}, bf16[512,2,128]{2,0,1:T(8,128)(2,1)S(1)}, u32[]{:S(2)}, u32[]{:S(2)}) collective-permute-start(bf16[512,2,128]{2,0,1:T(8,128)(2,1)S(1)} %constant_dynamic-update-slice_fusion), channel_id=1, source_target_pairs={{0,64},{16,80},{32,96},{48,112},{64,128},{80,144},{96,160},{112,17... | collective-permute-start | bytes 786440 | tf_op jit(solution)/shard_map/ppermute | solution.py:76
  15.9 34.0 %copy-start.10 = (s32[4608]{0:T(1024)}, s32[4608]{0:T(1024)S(1)}, u32[]{:S(2)}) copy-start(s32[4608]{0:T(1024)S(1)} %get-tuple-element.10) | copy-start | bytes 55300
  15.9 34.0 %copy-start.11 = (s32[4608]{0:T(1024)}, s32[4608]{0:T(1024)S(1)}, u32[]{:S(2)}) copy-start(s32[4608]{0:T(1024)S(1)} %get-tuple-element.11) | copy-start | bytes 55300
  16.7 31.0 %copy-start.17 = (bf16[512,1,128]{2,0,1:T(8,128)(2,1)S(1)}, bf16[512,1,128]{2,0,1:T(8,128)(2,1)}, u32[]{:S(2)}) copy-start(bf16[512,1,128]{2,0,1:T(8,128)(2,1)} %param.16) | copy-start | bytes 393220
  24.9 22.5 %collective-permute-start.5 = (bf16[512,2,128]{2,0,1:T(8,128)(2,1)S(1)}, bf16[512,2,128]{2,0,1:T(8,128)(2,1)S(1)}, u32[]{:S(2)}, u32[]{:S(2)}) collective-permute-start(bf16[512,2,128]{2,0,1:T(8,128)(2,1)S(1)} %constant_dynamic-update-slice_fusion), channel_id=1, source_target_pairs={{0,48},{16,64},{32,80},{48,96},{64,112},{80,128},{96,144},{112,160... | collective-permute-start | bytes 786440 | tf_op jit(solution)/shard_map/ppermute | solution.py:76
  27.0 20.5 %collective-permute-start.6 = (bf16[512,2,128]{2,0,1:T(8,128)(2,1)S(1)}, bf16[512,2,128]{2,0,1:T(8,128)(2,1)S(1)}, u32[]{:S(2)}, u32[]{:S(2)}) collective-permute-start(bf16[512,2,128]{2,0,1:T(8,128)(2,1)S(1)} %constant_dynamic-update-slice_fusion), channel_id=1, source_target_pairs={{0,32},{16,48},{32,64},{48,80},{64,96},{80,112},{96,128},{112,144}... | collective-permute-start | bytes 786440 | tf_op jit(solution)/shard_map/ppermute | solution.py:76
  30.9 16.7 %collective-permute-start.7 = (bf16[512,2,128]{2,0,1:T(8,128)(2,1)S(1)}, bf16[512,2,128]{2,0,1:T(8,128)(2,1)S(1)}, u32[]{:S(2)}, u32[]{:S(2)}) collective-permute-start(bf16[512,2,128]{2,0,1:T(8,128)(2,1)S(1)} %constant_dynamic-update-slice_fusion), channel_id=1, source_target_pairs={{0,16},{16,32},{32,48},{48,64},{64,80},{80,96},{96,112},{112,128},... | collective-permute-start | bytes 786440 | tf_op jit(solution)/shard_map/ppermute | solution.py:76
  47.7 2.2 copy-start.14
  49.9 3.6 copy-start.2
  67.6 55.4 %all-to-all-start = ((bf16[512,16,128]{2,0,1:T(8,128)(2,1)}), bf16[512,16,128]{2,0,1:T(8,128)(2,1)S(1)}, u32[]{:S(2)}, u32[]{:S(2)}) async-start(bf16[512,16,128]{2,0,1:T(8,128)(2,1)} %bitcast.219), calls=%async_computation | async-start | bytes 4194304 | tf_op jit(solution)/shard_map/all_to_all | solution.py:21
  123.2 0.7 copy-start.4
  126.6 8.0 %copy-start.15 = (s32[512,6]{0,1:T(8,128)S(1)}, s32[512,6]{0,1:T(8,128)}, u32[]{:S(2)}) copy-start(s32[512,6]{0,1:T(8,128)} %param.22) | copy-start | bytes 36868
  126.6 71.8 %all-to-all-start.1 = ((bf16[512,16,128]{2,0,1:T(8,128)(2,1)}), bf16[512,16,128]{2,0,1:T(8,128)(2,1)S(1)}, u32[]{:S(2)}, u32[]{:S(2)}) async-start(bf16[512,16,128]{2,0,1:T(8,128)(2,1)} %broadcast_in_dim.58), calls=%async_computation.1 | async-start | bytes 4194304 | tf_op jit(solution)/shard_map/all_to_all | solution.py:110
  198.4 1.3 copy-start.1
  210.5 58.1 %copy-start.16 = (bf16[352,2048]{1,0:T(8,128)(2,1)S(1)}, bf16[352,2048]{1,0:T(8,128)(2,1)}, u32[]{:S(2)}) copy-start(bf16[352,2048]{1,0:T(8,128)(2,1)} %param.24) | copy-start | bytes 4325380
  266.7 1.9 copy-start.3
  286.1 98.4 %all-to-all-start.4 = ((bf16[16,1,1024,128]{3,2,1,0:T(8,128)(2,1)}), bf16[16,1,1024,128]{3,2,1,0:T(8,128)(2,1)}, u32[]{:S(2)}, u32[]{:S(2)}) async-start(bf16[16,1,1024,128]{3,2,1,0:T(8,128)(2,1)} %bitcast.218), calls=%async_computation.4 | async-start | bytes 8388608 | tf_op jit(solution)/shard_map/all_to_all | solution.py:166
  384.5 45.4 %all-to-all-start.2 = ((bf16[512,16,128]{2,0,1:T(8,128)(2,1)}), bf16[512,16,128]{2,0,1:T(8,128)(2,1)S(1)}, u32[]{:S(2)}, u32[]{:S(2)}) async-start(bf16[512,16,128]{2,0,1:T(8,128)(2,1)} %bitcast.220), calls=%async_computation.2 | async-start | bytes 4194304 | tf_op jit(solution)/shard_map/all_to_all | solution.py:21
  400.5 77.2 %copy-start.12 = (s32[3072,1]{0,1:T(1,128)S(1)}, s32[3072,1]{0,1:T(1,128)}, u32[]{:S(2)}) copy-start(s32[3072,1]{0,1:T(1,128)} %get-tuple-element.5) | copy-start | bytes 36868
  429.8 62.7 %all-to-all-start.5 = ((bf16[4,16,64,128]{3,2,0,1:T(8,128)(2,1)}), bf16[4,16,64,128]{3,2,0,1:T(8,128)(2,1)}, u32[]{:S(2)}, u32[]{:S(2)}) async-start(bf16[4,16,64,128]{3,2,0,1:T(8,128)(2,1)} %copy.49), calls=%async_computation.5 | async-start | bytes 2097152 | tf_op jit(solution)/shard_map/all_to_all | solution.py:174
  478.3 15.6 %copy-start.13 = (s32[3072]{0:T(1024)S(1)}, s32[3072]{0:T(1024)}, u32[]{:S(2)}) copy-start(s32[3072]{0:T(1024)} %broadcast_clamp_fusion) | copy-start | bytes 36868
  493.9 10.4 %copy-start.9 = (bf16[512,6,1]{1,2,0:T(2,128)(2,1)S(1)}, bf16[512,6,1]{1,2,0:T(2,128)(2,1)}, u32[]{:S(2)}) copy-start(bf16[512,6,1]{1,2,0:T(2,128)(2,1)} %copy.52) | copy-start | bytes 18436
  503.1 3.2 copy-start.5
  503.1 3.2 copy-start.6
where the time goes:
time: 512 us; the launch traced here: 508 us
  waiting for transfers between devices  185 us (36%)
  starting transfers between devices  110 us (21%)
  local copies, waits for them, and re-layouts  65.4 us (13%)
  other arithmetic  59.1 us (12%)
  blocking collectives  56.2 us (11%)
  matrix products  31.2 us (6%)
    all_to_all x1, waiting for transfers between devices, on_device(): lax.all_to_all(down_part, 'hid', split_axis=0, concat_axis=0, tiled=True)  78.1 us
    all_to_all x2, waiting for transfers between devices, hid_scatter_sum(): lax.all_to_all(part.reshape(rows, hid_count, width // hid_count), 'hid',...  72.9 us
    all_to_all x1, blocking collectives, on_device(): lax.all_to_all(send_rows, 'seq', split_axis=0, concat_axis=0, tiled=True)  56.2 us
    all_to_all x1, starting transfers between devices, on_device(): lax.all_to_all(expert_out.reshape(local_experts, seq_count, CAP, col_coun...  46.1 us
    another operation x2, other arithmetic  36.4 us
    all_to_all x2, starting transfers between devices, hid_scatter_sum(): lax.all_to_all(part.reshape(rows, hid_count, width // hid_count), 'hid',...  23.9 us
    ppermute x8, starting transfers between devices, on_device(): blocks.append(lax.ppermute(both, 'seq', pairs))  22.6 us
    ppermute x8, waiting for transfers between devices, on_device(): blocks.append(lax.ppermute(both, 'seq', pairs))  20.9 us
  transfers between devices with their start and end apart: 13, of which 7 were waited for; matrix products, arithmetic and copies ran while one was open for 16% of the time, Pallas kernels for 0%

commit v1 on v0

--- a/solution.py
+++ b/solution.py
@@ -18,12 +18,15 @@
 
 def hid_scatter_sum(part, hid_count):
     rows, width = part.shape
-    got = lax.all_to_all(
-        part.reshape(rows, hid_count, width // hid_count),
-        "hid",
-        split_axis=1,
-        concat_axis=1,
-        tiled=True,
+    local_x = part.reshape(rows, hid_count, width // hid_count)
+    got = jnp.concatenate(
+        jax.lax.all_to_all(
+            jnp.stack(jnp.split(local_x, jax.lax.axis_size("hid"), axis=1)),
+            axis_name="hid",
+            split_axis=0,
+            concat_axis=0,
+        ),
+        axis=1,
     )
     return jnp.sum(got.astype(jnp.float32), axis=1)
 

time: 512 us -> 527 us (1.029)
  local copies, waits for them, and re-layouts: 65.4 us -> 84.9 us
    unnamed x48 -> x86, local copies, waits for them, and re-layouts: 11 us -> 25.7 us
    split x0 -> x2, local copies, waits for them, and re-layouts: none -> 9.16 us  [hid_scatter_sum(): jnp.split(local_x, jax.lax.axis_size('hid'), axis=1)]
    reshape x2 -> x0, local copies, waits for them, and re-layouts: 5.37 us -> none  [hid_scatter_sum(): part.reshape(rows, hid_count, width // hid_count)]
    all_to_all x1, waiting for transfers between devices: 78.1 us -> 72.9 us  [on_device(): lax.all_to_all(down_part, 'hid', split_axis=0, concat_axis=0, tiled=True)]
  transfers between devices with their start and end apart: 13 -> 13, of which waited for: 7 -> 7; matrix products, arithmetic and copies ran while one was open for 16% -> 17% of each run, Pallas kernels for 0% -> 0%
where the time goes in v1:
time: 527 us; the launch traced here: 522 us
  waiting for transfers between devices  181 us (34%)
  starting transfers between devices  110 us (21%)
  local copies, waits for them, and re-layouts  84.9 us (16%)
  other arithmetic  59 us (11%)
  blocking collectives  55.9 us (11%)
  matrix products  31.2 us (6%)
    all_to_all x2, waiting for transfers between devices, hid_scatter_sum(): jax.lax.all_to_all(jnp.stack(jnp.split(local_x, jax.lax.axis_size('hid'),...  73.6 us
    all_to_all x1, waiting for transfers between devices, on_device(): lax.all_to_all(down_part, 'hid', split_axis=0, concat_axis=0, tiled=True)  72.9 us
    all_to_all x1, blocking collectives, on_device(): lax.all_to_all(send_rows, 'seq', split_axis=0, concat_axis=0, tiled=True)  55.9 us
    all_to_all x1, starting transfers between devices, on_device(): lax.all_to_all(expert_out.reshape(local_experts, seq_count, CAP, col_coun...  46.1 us
    another operation x2, other arithmetic  36.3 us
    unnamed x86, local copies, waits for them, and re-layouts  25.7 us
    all_to_all x2, starting transfers between devices, hid_scatter_sum(): jax.lax.all_to_all(jnp.stack(jnp.split(local_x, jax.lax.axis_size('hid'),...  23.9 us
    ppermute x8, starting transfers between devices, on_device(): blocks.append(lax.ppermute(both, 'seq', pairs))  22.6 us
  transfers between devices with their start and end apart: 13, of which 7 were waited for; matrix products, arithmetic and copies ran while one was open for 17% of the time, Pallas kernels for 0%

profile of v1, /device:TPU:64, one launch (start us, length us, event | category | flops | bytes accessed | tf_op | source)
XLA Modules:
  0.0 522.1 jit_solution(1454931714254336892)
XLA Ops:
  2.0 4.9 collective-permute-start
  6.9 3.0 collective-permute-start.1
  9.9 2.1 collective-permute-start.2
  16.6 8.2 %collective-permute-done = bf16[512,2,128]{2,0,1:T(8,128)(2,1)S(1)} collective-permute-done((bf16[512,2,128]{2,0,1:T(8,128)(2,1)S(1)}, bf16[512,2,128]{2,0,1:T(8,128)(2,1)S(1)}, u32[]{:S(2)}, u32[]{:S(2)}) %collective-permute-start) | collective-permute-done | bytes 262176 | tf_op jit(solution)/shard_map/ppermute | solution.py:79
  24.8 2.0 collective-permute-start.5
  26.9 4.0 collective-permute-start.6
  31.0 3.6 collective-permute-start.7
  34.6 7.1 %collective-permute-done.3 = bf16[512,2,128]{2,0,1:T(8,128)(2,1)S(1)} collective-permute-done((bf16[512,2,128]{2,0,1:T(8,128)(2,1)S(1)}, bf16[512,2,128]{2,0,1:T(8,128)(2,1)S(1)}, u32[]{:S(2)}, u32[]{:S(2)}) %collective-permute-start.3) | collective-permute-done | bytes 262176 | tf_op jit(solution)/shard_map/ppermute | solution.py:79
  41.7 5.6 %collective-permute-done.4 = bf16[512,2,128]{2,0,1:T(8,128)(2,1)S(1)} collective-permute-done((bf16[512,2,128]{2,0,1:T(8,128)(2,1)S(1)}, bf16[512,2,128]{2,0,1:T(8,128)(2,1)S(1)}, u32[]{:S(2)}, u32[]{:S(2)}) %collective-permute-start.4) | collective-permute-done | bytes 262176 | tf_op jit(solution)/shard_map/ppermute | solution.py:79
  47.6 2.2 fusion
  49.8 3.6 copy-done.2
  53.4 4.1 fusion.1
  57.6 8.1 %fusion.13 = bf16[64,8,16,128]{3,1,2,0:T(8,128)(2,1)S(1)} fusion(f32[4608,512]{1,0:T(8,128)} %copy-done.2, f32[512]{0:T(512)S(1)} %broadcast_maximum_fusion, s32[512]{0:T(512)S(1)} %iota_add_fusion.1, s32[512]{0:T(512)S(1)} %dynamic_slice.10, s32[4608]{0:T(1024)} %copy-done.12, s32[4608]{0:T(1024)} %copy-done.11, bf16[4608,2,128]{2,0,1:T(8,128)(2,1)} %copy-done.15, ...), kind=kOutput, calls=%fused_computation.28 | convolution fusion | flops 892469248 | bytes 13287424 | tf_op jit(solution)/shard_map/dot_general | solution.py:106
  66.2 4.6 fusion.109
  81.5 10.8 %all-to-all-start = ((bf16[16,512,1,128]{3,1,2,0:T(8,128)(2,1)}), bf16[16,512,1,128]{3,1,2,0:T(8,128)(2,1)S(1)}, u32[]{:S(2)}, u32[]{:S(2)}) async-start(bf16[16,512,1,128]{3,1,2,0:T(8,128)(2,1)} %fusion.77), calls=%async_computation | async-start | bytes 4194304 | tf_op jit(solution)/shard_map/all_to_all | solution.py:23
  92.3 45.3 %all-to-all-done = bf16[16,512,1,128]{3,1,2,0:T(8,128)(2,1)S(1)} async-done(((bf16[16,512,1,128]{3,1,2,0:T(8,128)(2,1)}), bf16[16,512,1,128]{3,1,2,0:T(8,128)(2,1)S(1)}, u32[]{:S(2)}, u32[]{:S(2)}) %all-to-all-start) | async-done | bytes 2097184 | tf_op jit(solution)/shard_map/all_to_all | solution.py:23
  139.5 1.7 broadcast_in_dim.58
  141.3 7.4 %all-to-all-start.1 = ((bf16[512,16,128]{2,0,1:T(8,128)(2,1)}), bf16[512,16,128]{2,0,1:T(8,128)(2,1)S(1)}, u32[]{:S(2)}, u32[]{:S(2)}) async-start(bf16[512,16,128]{2,0,1:T(8,128)(2,1)} %broadcast_in_dim.58), calls=%async_computation.1 | async-start | bytes 4194304 | tf_op jit(solution)/shard_map/all_to_all | solution.py:113
  149.6 1.7 eq.54
  151.3 1.7 eq.50
  154.2 1.6 fusion.50
  155.8 34.8 %reduce-window.6 = s32[64,24,128]{2,1,0:T(8,128)} reduce-window(s32[64,24,128]{2,1,0:T(8,128)} %fusion.50, s32[]{:T(128)} %constant.41.clone.1), window={size=1x1x128 pad=0_0x0_0x127_0}, to_apply=%region_5.6 | reduce-window | flops 24969216 | bytes 1572868 | tf_op jit(solution)/shard_map/reduce-window
  190.6 2.3 slice.22
  192.9 2.2 copy.176
  200.3 11.9 %scatter_custom_fusion = s32[1024]{0:T(1024)S(1)} fusion(s32[3072]{0:T(1024)S(1)} %bitcast.354, s32[3072]{0:T(1024)} %add_select_fusion, s32[]{:T(128)} %constant.86.clone.1), kind=kCustom, calls=%fused_computation.167 | custom fusion | bytes 4608 | tf_op jit(solution)/shard_map/scatter | solution.py:151
  214.3 2.1 fusion.8
  216.4 6.0 %gather_fusion = bf16[1024,2048]{1,0:T(8,128)(2,1)} fusion(bf16[512,2048]{1,0:T(8,128)(2,1)S(1)} %fusion.8, s32[1024]{0:T(1024)S(1)} %maximum_clamp_fusion), kind=kCustom, calls=%fused_computation | custom fusion | bytes 8392704 | tf_op jit(solution)/shard_map/gather | solution.py:153
  222.5 2.5 broadcast_select_fusion
  225.0 55.9 %all_to_all.30 = bf16[16,1,64,2048]{3,2,1,0:T(8,128)(2,1)S(1)} all-to-all(bf16[16,1,64,2048]{3,2,1,0:T(8,128)(2,1)S(1)} %broadcast_select_fusion), channel_id=1, replica_groups=mesh['seq'=16,'hid'=16] {'seq'}, dimensions={0} | all-to-all | bytes 8388608 | tf_op jit(solution)/shard_map/all_to_all | solution.py:156
  280.9 2.0 copy-done.3
  282.9 3.6 fusion.11
  286.4 8.4 %convert_bitcast_fusion.1 = bf16[16,1,16,64,128]{4,3,0,2,1:T(8,128)(2,1)} fusion(bf16[352,2048]{1,0:T(8,128)(2,1)S(1)} %copy-done, bf16[16,1,64,2048]{3,2,1,0:T(8,128)(2,1)} %copy-done.3, f32[16,64,352]{2,1,0:T(8,128)} %fusion.11, bf16[352,2048]{1,0:T(8,128)(2,1)} %param.26), kind=kOutput, calls=%fused_computation.22 | convolution fusion | flops 2957049856 | bytes 12713984 | tf_op jit(solution)/shard_map/sicf,ifnx->niscx/dot_general | solution.py:165
  294.8 5.5 %copy.169 = bf16[16,1,16,64,128]{4,3,2,0,1:T(8,128)(2,1)} copy(bf16[16,1,16,64,128]{4,3,0,2,1:T(8,128)(2,1)} %convert_bitcast_fusion.1) | data formatting | bytes 8388608 | tf_op jit(solution)/shard_map/convert_element_type | solution.py:167
  300.3 9.6 %all-to-all-start.4 = ((bf16[16,1,1024,128]{3,2,1,0:T(8,128)(2,1)}), bf16[16,1,1024,128]{3,2,1,0:T(8,128)(2,1)}, u32[]{:S(2)}, u32[]{:S(2)}) async-start(bf16[16,1,1024,128]{3,2,1,0:T(8,128)(2,1)} %bitcast.344), calls=%async_computation.4 | async-start | bytes 8388608 | tf_op jit(solution)/shard_map/all_to_all | solution.py:169
  310.0 2.7 fusion.110
  312.7 4.4 fusion.14
  317.1 2.2 copy.212
  319.3 4.6 fusion.108
  325.8 72.9 %all-to-all-done.4 = bf16[16,1,1024,128]{3,2,1,0:T(8,128)(2,1)} async-done(((bf16[16,1,1024,128]{3,2,1,0:T(8,128)(2,1)}), bf16[16,1,1024,128]{3,2,1,0:T(8,128)(2,1)}, u32[]{:S(2)}, u32[]{:S(2)}) %all-to-all-start.4) | async-done | bytes 4194336 | tf_op jit(solution)/shard_map/all_to_all | solution.py:169
  398.7 13.2 %all-to-all-start.2 = ((bf16[16,512,1,128]{3,1,2,0:T(8,128)(2,1)}), bf16[16,512,1,128]{3,1,2,0:T(8,128)(2,1)S(1)}, u32[]{:S(2)}, u32[]{:S(2)}) async-start(bf16[16,512,1,128]{3,1,2,0:T(8,128)(2,1)} %copy-done.4), calls=%async_computation.2 | async-start | bytes 4194304 | tf_op jit(solution)/shard_map/all_to_all | solution.py:23
  411.9 2.9 bitcast_reduce_fusion
  415.8 28.3 %all-to-all-done.2 = bf16[16,512,1,128]{3,1,2,0:T(8,128)(2,1)S(1)} async-done(((bf16[16,512,1,128]{3,1,2,0:T(8,128)(2,1)}), bf16[16,512,1,128]{3,1,2,0:T(8,128)(2,1)S(1)}, u32[]{:S(2)}, u32[]{:S(2)}) %all-to-all-start.2) | async-done | bytes 2097184 | tf_op jit(solution)/shard_map/all_to_all | solution.py:23
  444.1 46.1 %all-to-all-start.5 = ((bf16[4,16,64,128]{3,2,0,1:T(8,128)(2,1)}), bf16[4,16,64,128]{3,2,0,1:T(8,128)(2,1)}, u32[]{:S(2)}, u32[]{:S(2)}) async-start(bf16[4,16,64,128]{3,2,0,1:T(8,128)(2,1)} %copy.171), calls=%async_computation.5 | async-start | bytes 2097152 | tf_op jit(solution)/shard_map/all_to_all | solution.py:177
  490.2 1.7 copy.174
  493.5 13.3 %all-to-all-done.5 = bf16[4,16,64,128]{3,2,0,1:T(8,128)(2,1)} async-done(((bf16[4,16,64,128]{3,2,0,1:T(8,128)(2,1)}), bf16[4,16,64,128]{3,2,0,1:T(8,128)(2,1)}, u32[]{:S(2)}, u32[]{:S(2)}) %all-to-all-start.5) | async-done | bytes 1048608 | tf_op jit(solution)/shard_map/all_to_all | solution.py:177
  508.2 9.2 %gather_fusion.1 = bf16[3072,128]{1,0:T(8,128)(2,1)S(1)} fusion(bf16[4096,128]{1,0:T(8,128)(2,1)S(1)} %bitcast.340, s32[3072]{0:T(1024)S(1)} %copy-done.14), kind=kCustom, calls=%fused_computation.1 | custom fusion | bytes 1585152 | tf_op jit(solution)/shard_map/gather | solution.py:185
  518.6 1.9 fusion.111
  520.5 1.6 add_convert_fusion
  (117 shorter events, 36.3 us)
Async XLA Ops:
  0.0 286.4 %copy-start = (bf16[352,2048]{1,0:T(8,128)(2,1)S(1)}, bf16[352,2048]{1,0:T(8,128)(2,1)}, u32[]{:S(2)}) copy-start(bf16[352,2048]{1,0:T(8,128)(2,1)} %param.25) | copy-start | bytes 4325380
  2.0 22.9 %collective-permute-start = (bf16[512,2,128]{2,0,1:T(8,128)(2,1)S(1)}, bf16[512,2,128]{2,0,1:T(8,128)(2,1)S(1)}, u32[]{:S(2)}, u32[]{:S(2)}) collective-permute-start(bf16[512,2,128]{2,0,1:T(8,128)(2,1)S(1)} %constant_dynamic-update-slice_fusion), channel_id=1, source_target_pairs={{0,128},{16,144},{32,160},{48,176},{64,192},{80,208},{96,224},{112... | collective-permute-start | bytes 786440 | tf_op jit(solution)/shard_map/ppermute | solution.py:79
  6.9 20.0 %collective-permute-start.1 = (bf16[512,2,128]{2,0,1:T(8,128)(2,1)S(1)}, bf16[512,2,128]{2,0,1:T(8,128)(2,1)S(1)}, u32[]{:S(2)}, u32[]{:S(2)}) collective-permute-start(bf16[512,2,128]{2,0,1:T(8,128)(2,1)S(1)} %constant_dynamic-update-slice_fusion), channel_id=1, source_target_pairs={{0,112},{16,128},{32,144},{48,160},{64,176},{80,192},{96,208},{112... | collective-permute-start | bytes 786440 | tf_op jit(solution)/shard_map/ppermute | solution.py:79
  9.9 21.0 %collective-permute-start.2 = (bf16[512,2,128]{2,0,1:T(8,128)(2,1)S(1)}, bf16[512,2,128]{2,0,1:T(8,128)(2,1)S(1)}, u32[]{:S(2)}, u32[]{:S(2)}) collective-permute-start(bf16[512,2,128]{2,0,1:T(8,128)(2,1)S(1)} %constant_dynamic-update-slice_fusion), channel_id=1, source_target_pairs={{0,96},{16,112},{32,128},{48,144},{64,160},{80,176},{96,192},{112,... | collective-permute-start | bytes 786440 | tf_op jit(solution)/shard_map/ppermute | solution.py:79
  12.1 29.6 %collective-permute-start.3 = (bf16[512,2,128]{2,0,1:T(8,128)(2,1)S(1)}, bf16[512,2,128]{2,0,1:T(8,128)(2,1)S(1)}, u32[]{:S(2)}, u32[]{:S(2)}) collective-permute-start(bf16[512,2,128]{2,0,1:T(8,128)(2,1)S(1)} %constant_dynamic-update-slice_fusion), channel_id=1, source_target_pairs={{0,80},{16,96},{32,112},{48,128},{64,144},{80,160},{96,176},{112,1... | collective-permute-start | bytes 786440 | tf_op jit(solution)/shard_map/ppermute | solution.py:79
  13.4 33.9 %collective-permute-start.4 = (bf16[512,2,128]{2,0,1:T(8,128)(2,1)S(1)}, bf16[512,2,128]{2,0,1:T(8,128)(2,1)S(1)}, u32[]{:S(2)}, u32[]{:S(2)}) collective-permute-start(bf16[512,2,128]{2,0,1:T(8,128)(2,1)S(1)} %constant_dynamic-update-slice_fusion), channel_id=1, source_target_pairs={{0,64},{16,80},{32,96},{48,112},{64,128},{80,144},{96,160},{112,17... | collective-permute-start | bytes 786440 | tf_op jit(solution)/shard_map/ppermute | solution.py:79
  15.8 34.0 %copy-start.11 = (s32[4608]{0:T(1024)}, s32[4608]{0:T(1024)S(1)}, u32[]{:S(2)}) copy-start(s32[4608]{0:T(1024)S(1)} %get-tuple-element.42) | copy-start | bytes 55300
  15.8 34.0 %copy-start.12 = (s32[4608]{0:T(1024)}, s32[4608]{0:T(1024)S(1)}, u32[]{:S(2)}) copy-start(s32[4608]{0:T(1024)S(1)} %get-tuple-element.43) | copy-start | bytes 55300
  16.6 30.9 %copy-start.8 = (bf16[512,1,128]{2,0,1:T(8,128)(2,1)S(1)}, bf16[512,1,128]{2,0,1:T(8,128)(2,1)}, u32[]{:S(2)}) copy-start(bf16[512,1,128]{2,0,1:T(8,128)(2,1)} %param.17) | copy-start | bytes 393220
  24.8 22.5 %collective-permute-start.5 = (bf16[512,2,128]{2,0,1:T(8,128)(2,1)S(1)}, bf16[512,2,128]{2,0,1:T(8,128)(2,1)S(1)}, u32[]{:S(2)}, u32[]{:S(2)}) collective-permute-start(bf16[512,2,128]{2,0,1:T(8,128)(2,1)S(1)} %constant_dynamic-update-slice_fusion), channel_id=1, source_target_pairs={{0,48},{16,64},{32,80},{48,96},{64,112},{80,128},{96,144},{112,160... | collective-permute-start | bytes 786440 | tf_op jit(solution)/shard_map/ppermute | solution.py:79
  26.9 20.7 %copy-start.9 = (bf16[512,1,128]{2,0,1:T(8,128)(2,1)S(1)}, bf16[512,1,128]{2,0,1:T(8,128)(2,1)}, u32[]{:S(2)}) copy-start(bf16[512,1,128]{2,0,1:T(8,128)(2,1)} %param.18) | copy-start | bytes 393220
  26.9 20.7 %copy-start.20 = (bf16[512,1,128]{2,0,1:T(8,128)(2,1)S(1)}, bf16[512,1,128]{2,0,1:T(8,128)(2,1)}, u32[]{:S(2)}) copy-start(bf16[512,1,128]{2,0,1:T(8,128)(2,1)} %param.16) | copy-start | bytes 393220
  26.9 20.5 %collective-permute-start.6 = (bf16[512,2,128]{2,0,1:T(8,128)(2,1)S(1)}, bf16[512,2,128]{2,0,1:T(8,128)(2,1)S(1)}, u32[]{:S(2)}, u32[]{:S(2)}) collective-permute-start(bf16[512,2,128]{2,0,1:T(8,128)(2,1)S(1)} %constant_dynamic-update-slice_fusion), channel_id=1, source_target_pairs={{0,32},{16,48},{32,64},{48,80},{64,96},{80,112},{96,128},{112,144}... | collective-permute-start | bytes 786440 | tf_op jit(solution)/shard_map/ppermute | solution.py:79
  31.0 16.5 %collective-permute-start.7 = (bf16[512,2,128]{2,0,1:T(8,128)(2,1)S(1)}, bf16[512,2,128]{2,0,1:T(8,128)(2,1)S(1)}, u32[]{:S(2)}, u32[]{:S(2)}) collective-permute-start(bf16[512,2,128]{2,0,1:T(8,128)(2,1)S(1)} %constant_dynamic-update-slice_fusion), channel_id=1, source_target_pairs={{0,16},{16,32},{32,48},{48,64},{64,80},{80,96},{96,112},{112,128},... | collective-permute-start | bytes 786440 | tf_op jit(solution)/shard_map/ppermute | solution.py:79
  47.6 2.2 copy-start.15
  49.8 3.7 copy-start.2
  81.5 56.1 %all-to-all-start = ((bf16[16,512,1,128]{3,1,2,0:T(8,128)(2,1)}), bf16[16,512,1,128]{3,1,2,0:T(8,128)(2,1)S(1)}, u32[]{:S(2)}, u32[]{:S(2)}) async-start(bf16[16,512,1,128]{3,1,2,0:T(8,128)(2,1)} %fusion.77), calls=%async_computation | async-start | bytes 4194304 | tf_op jit(solution)/shard_map/all_to_all | solution.py:23
  137.9 0.7 copy-start.5
  141.3 7.4 %copy-start.16 = (s32[512,6]{0,1:T(8,128)S(1)}, s32[512,6]{0,1:T(8,128)}, u32[]{:S(2)}) copy-start(s32[512,6]{0,1:T(8,128)} %param.22) | copy-start | bytes 36868
  141.3 71.6 %all-to-all-start.1 = ((bf16[512,16,128]{2,0,1:T(8,128)(2,1)}), bf16[512,16,128]{2,0,1:T(8,128)(2,1)S(1)}, u32[]{:S(2)}, u32[]{:S(2)}) async-start(bf16[512,16,128]{2,0,1:T(8,128)(2,1)} %broadcast_in_dim.58), calls=%async_computation.1 | async-start | bytes 4194304 | tf_op jit(solution)/shard_map/all_to_all | solution.py:113
  212.2 2.0 copy-start.17
  212.9 1.3 copy-start.1
  216.4 6.0 %copy-start.18 = (pred[16,64]{1,0:T(8,128)(4,1)S(1)}, pred[16,64]{1,0:T(8,128)(4,1)}, u32[]{:S(2)}) copy-start(pred[16,64]{1,0:T(8,128)(4,1)} %broadcast_in_dim.61) | copy-start | bytes 3076
  225.0 57.9 %copy-start.19 = (bf16[352,2048]{1,0:T(8,128)(2,1)S(1)}, bf16[352,2048]{1,0:T(8,128)(2,1)}, u32[]{:S(2)}) copy-start(bf16[352,2048]{1,0:T(8,128)(2,1)} %param.24) | copy-start | bytes 4325380
  280.9 2.0 copy-start.3
  300.3 98.4 %all-to-all-start.4 = ((bf16[16,1,1024,128]{3,2,1,0:T(8,128)(2,1)}), bf16[16,1,1024,128]{3,2,1,0:T(8,128)(2,1)}, u32[]{:S(2)}, u32[]{:S(2)}) async-start(bf16[16,1,1024,128]{3,2,1,0:T(8,128)(2,1)} %bitcast.344), calls=%async_computation.4 | async-start | bytes 8388608 | tf_op jit(solution)/shard_map/all_to_all | solution.py:169
  324.5 1.4 copy-start.4
  398.7 45.4 %all-to-all-start.2 = ((bf16[16,512,1,128]{3,1,2,0:T(8,128)(2,1)}), bf16[16,512,1,128]{3,1,2,0:T(8,128)(2,1)S(1)}, u32[]{:S(2)}, u32[]{:S(2)}) async-start(bf16[16,512,1,128]{3,1,2,0:T(8,128)(2,1)} %copy-done.4), calls=%async_computation.2 | async-start | bytes 4194304 | tf_op jit(solution)/shard_map/all_to_all | solution.py:23
  414.7 77.2 %copy-start.13 = (s32[3072,1]{0,1:T(1,128)S(1)}, s32[3072,1]{0,1:T(1,128)}, u32[]{:S(2)}) copy-start(s32[3072,1]{0,1:T(1,128)} %get-tuple-element.5) | copy-start | bytes 36868
  444.1 62.7 %all-to-all-start.5 = ((bf16[4,16,64,128]{3,2,0,1:T(8,128)(2,1)}), bf16[4,16,64,128]{3,2,0,1:T(8,128)(2,1)}, u32[]{:S(2)}, u32[]{:S(2)}) async-start(bf16[4,16,64,128]{3,2,0,1:T(8,128)(2,1)} %copy.171), calls=%async_computation.5 | async-start | bytes 2097152 | tf_op jit(solution)/shard_map/all_to_all | solution.py:177
  492.5 15.6 %copy-start.14 = (s32[3072]{0:T(1024)S(1)}, s32[3072]{0:T(1024)}, u32[]{:S(2)}) copy-start(s32[3072]{0:T(1024)} %broadcast_clamp_fusion) | copy-start | bytes 36868
  508.2 10.4 %copy-start.10 = (bf16[512,6,1]{1,2,0:T(2,128)(2,1)S(1)}, bf16[512,6,1]{1,2,0:T(2,128)(2,1)}, u32[]{:S(2)}) copy-start(bf16[512,6,1]{1,2,0:T(2,128)(2,1)} %copy.174) | copy-start | bytes 18436
  517.3 3.2 copy-start.6
  517.3 3.2 copy-start.7
